TPU v7x, 256 devices: a whole 4x4x8 slice. The times are simulated.
256 devices in a mesh: dp: 8 (over z_hi, x), seq: 32 (over y, z_lo, core).
Axes of the slice: x: 4, y: 4, z: 8 (z_hi: 2, z_lo: 4; z = z_hi * 4 + z_lo), core: 2. Of those that a mesh axis runs over, the one named last changes fastest.
Arguments:
- inputs: bfloat16 [8, 32768, 1024], P('dp', 'seq'), may hold values from -6 to 6
- cotangent: bfloat16 [8, 32768, 1024], P('dp', 'seq'), may hold values from -4 to 4
- factor_one: bfloat16 [32, 1024, 1024], P('seq'), may hold values from -0.1875 to 0.1875
- factor_two: bfloat16 [32, 1024, 1024], P('seq'), may hold values from -0.1875 to 0.1875
Outputs:
- mixed: bfloat16 [8, 32768, 1024], P('dp', 'seq')
- grad_input: bfloat16 [8, 32768, 1024], P('dp', 'seq')
- grad_one: float32 [32, 1024, 1024], P('seq', 'dp')
- grad_two: float32 [32, 1024, 1024], P('seq', 'dp')
All inputs are finite; a program needn't handle non-finite values.
Results may differ from a plain program's by a relative error of at most 0.014.
Values may be sent and summed in bfloat16 or wider, within the bound.
No kernel may reach another device: no remote copies, remote signals or barrier semaphores. Data moves between devices by JAX's collectives and lax.ppermute only.
A program may use at most 128 MiB of HBM per device.

v0:
```python
import jax
import jax.numpy as jnp
from jax import lax
from jax.sharding import PartitionSpec as P


def local(inputs, cotangent, factor_one, factor_two):
    seqs, block, width = inputs.shape
    count = lax.axis_size("seq")
    rows = block // count
    fone = factor_one[0]
    ftwo = factor_two[0]
    xfull = inputs.astype(jnp.float32)
    dyfull = cotangent.astype(jnp.float32)
    first = jnp.einsum("kj,sjc->skc", fone, inputs, preferred_element_type=jnp.float32).astype(
        jnp.bfloat16
    )
    gated = (dyfull * xfull).astype(jnp.bfloat16)
    moved = lax.all_to_all(
        first.reshape(seqs, count, rows, 1, width), "seq", split_axis=1, concat_axis=3, tiled=True
    )
    moved = moved.reshape(seqs, block, width)
    second = jnp.einsum("pq,sqc->spc", ftwo, moved, preferred_element_type=jnp.float32).astype(
        jnp.bfloat16
    )
    monarch = lax.all_to_all(
        second.reshape(seqs, 1, rows, count, width), "seq", split_axis=3, concat_axis=1, tiled=True
    )
    monarch = monarch.reshape(seqs, block, width)
    gated_moved = lax.all_to_all(
        gated.reshape(seqs, count, rows, 1, width), "seq", split_axis=1, concat_axis=3, tiled=True
    )
    gated_moved = gated_moved.reshape(seqs, block, width)
    back_two = jnp.einsum(
        "pq,spc->sqc", ftwo, gated_moved, preferred_element_type=jnp.float32
    ).astype(jnp.bfloat16)
    back_moved = lax.all_to_all(
        back_two.reshape(seqs, 1, rows, count, width),
        "seq",
        split_axis=3,
        concat_axis=1,
        tiled=True,
    )
    back_moved = back_moved.reshape(seqs, block, width)
    mfull = monarch.astype(jnp.float32)
    mixed = (xfull * mfull).astype(jnp.bfloat16)
    part_two = jnp.einsum("spc,sqc->pq", gated_moved, moved, preferred_element_type=jnp.float32)
    part_one = jnp.einsum("skc,sjc->kj", back_moved, inputs, preferred_element_type=jnp.float32)
    grad_one, grad_two = (
        lax.psum_scatter(
            part_one.astype(jnp.bfloat16), "dp", scatter_dimension=0, tiled=True
        ).astype(jnp.float32),
        lax.psum_scatter(
            part_two.astype(jnp.bfloat16), "dp", scatter_dimension=0, tiled=True
        ).astype(jnp.float32),
    )
    spread = jnp.einsum("kj,skc->sjc", fone, back_moved, preferred_element_type=jnp.float32)
    grad_input = (dyfull * mfull + spread).astype(jnp.bfloat16)
    return (mixed, grad_input, grad_one[None], grad_two[None])


def solution(mesh):
    in_specs = (
        P("dp", "seq", None),
        P("dp", "seq", None),
        P("seq", None, None),
        P("seq", None, None),
    )
    out_specs = (
        P("dp", "seq", None),
        P("dp", "seq", None),
        P("seq", "dp", None),
        P("seq", "dp", None),
    )
    return jax.shard_map(local, mesh=mesh, in_specs=in_specs, out_specs=out_specs, check_vma=False)
```

profile of v0, /device:TPU:8, one launch (start us, length us, event | category | flops | bytes accessed | tf_op | source)
XLA Modules:
  0.0 429.8 jit_solution(16111633440075535005)
XLA Ops:
  7.2 4.7 %fusion.17 = bf16[1024,1024]{0,1:T(8,128)(2,1)S(1)} fusion(bf16[1,1024,1024]{2,1,0:T(8,128)(2,1)} %param.4, bf16[1,1024,1024]{2,1,0:T(8,128)(2,1)} %param.6), kind=kOutput, calls=%fused_computation.19 | convolution fusion | flops 2148532224 | bytes 6291456 | tf_op jit(solution)/shard_map/kj,sjc->skc/dot_general | solution.py:15
  11.9 56.7 %all_to_all.54 = bf16[1,32,32,1,1024]{4,2,3,0,1:T(8,128)(2,1)S(1)} all-to-all(bf16[1,32,32,1,1024]{4,2,3,0,1:T(8,128)(2,1)S(1)} %bitcast.90), channel_id=1, replica_groups=mesh['dp'=8,'seq'=32] {'seq'}, dimensions={1} | all-to-all | bytes 4194304 | tf_op jit(solution)/shard_map/all_to_all | solution.py:19
  69.8 2.4 fusion.22
  72.2 2.5 copy.27
  74.6 7.2 %all-to-all-start.1 = ((bf16[1,1,32,32,1024]{4,2,1,0,3:T(8,128)(2,1)}), bf16[1,1,32,32,1024]{4,2,1,0,3:T(8,128)(2,1)}, u32[]{:S(2)}, u32[]{:S(2)}) async-start(bf16[1,1,32,32,1024]{4,2,1,0,3:T(8,128)(2,1)} %copy.27), calls=%async_computation.1 | async-start | bytes 4194304 | tf_op jit(solution)/shard_map/all_to_all | solution.py:26
  81.8 3.9 copy.24
  85.7 3.9 copy.30
  89.7 40.1 %all-to-all-done.1 = bf16[1,1,32,32,1024]{4,2,1,0,3:T(8,128)(2,1)} async-done(((bf16[1,1,32,32,1024]{4,2,1,0,3:T(8,128)(2,1)}), bf16[1,1,32,32,1024]{4,2,1,0,3:T(8,128)(2,1)}, u32[]{:S(2)}, u32[]{:S(2)}) %all-to-all-start.1) | async-done | bytes 2097184 | tf_op jit(solution)/shard_map/all_to_all | solution.py:26
  129.7 4.1 bitcast_convert_fusion
  133.8 5.3 %copy.29 = f32[1,1024,1024]{1,2,0:T(8,128)} copy(f32[1,1024,1024]{2,1,0:T(8,128)} %bitcast.84) | data formatting | bytes 8388608 | tf_op jit(solution)/shard_map/convert_element_type | solution.py:45
  139.1 6.9 %fusion.3 = (bf16[1,1024,1024]{1,2,0:T(8,128)(2,1)}, bf16[1,1024,1024]{1,2,0:T(8,128)(2,1)}) fusion(bf16[1,1024,1024]{1,2,0:T(8,128)(2,1)} %copy.24, bf16[1,1024,1024]{1,2,0:T(8,128)(2,1)} %copy.30, f32[1,1024,1024]{1,2,0:T(8,128)} %copy.29), kind=kLoop, calls=%fused_computation.6 | loop fusion | flops 6291456 | bytes 12582912 | tf_op jit(solution)/shard_map/convert_element_type | solution.py:18
  146.0 3.9 copy.32
  149.9 54.3 %all_to_all.55 = bf16[1,32,32,1,1024]{4,2,3,0,1:T(8,128)(2,1)S(1)} all-to-all(bf16[1,32,32,1,1024]{4,2,3,0,1:T(8,128)(2,1)} %bitcast.85), channel_id=1, replica_groups=mesh['dp'=8,'seq'=32] {'seq'}, dimensions={1} | all-to-all | bytes 4194304 | tf_op jit(solution)/shard_map/all_to_all | solution.py:30
  205.4 2.4 fusion.25
  207.9 2.5 copy.35
  210.3 7.2 %all-to-all-start.3 = ((bf16[1,1,32,32,1024]{4,2,1,0,3:T(8,128)(2,1)}), bf16[1,1,32,32,1024]{4,2,1,0,3:T(8,128)(2,1)}, u32[]{:S(2)}, u32[]{:S(2)}) async-start(bf16[1,1,32,32,1024]{4,2,1,0,3:T(8,128)(2,1)} %copy.35), calls=%async_computation.3 | async-start | bytes 4194304 | tf_op jit(solution)/shard_map/all_to_all | solution.py:37
  217.6 5.9 %convolution_convert_fusion = bf16[1024,1024]{1,0:T(8,128)(2,1)} fusion(bf16[1024,1024]{1,0:T(8,128)(2,1)} %bitcast.89, bf16[1024,1024]{1,0:T(8,128)(2,1)} %bitcast.87), kind=kOutput, calls=%fused_computation.22 | convolution fusion | flops 2148532224 | bytes 6291456 | tf_op jit(solution)/shard_map/spc,sqc->pq/dot_general | solution.py:47
  223.8 59.9 %all-to-all-done.3 = bf16[1,1,32,32,1024]{4,2,1,0,3:T(8,128)(2,1)} async-done(((bf16[1,1,32,32,1024]{4,2,1,0,3:T(8,128)(2,1)}), bf16[1,1,32,32,1024]{4,2,1,0,3:T(8,128)(2,1)}, u32[]{:S(2)}, u32[]{:S(2)}) %all-to-all-start.3) | async-done | bytes 2097184 | tf_op jit(solution)/shard_map/all_to_all | solution.py:37
  283.8 5.9 %fusion.14 = bf16[1024,1024]{1,0:T(8,128)(2,1)} fusion(bf16[1024,1024]{1,0:T(8,128)(2,1)} %bitcast.29, bf16[1,1024,1024]{2,1,0:T(8,128)(2,1)} %param.4), kind=kOutput, calls=%fused_computation.18 | convolution fusion | flops 2148532224 | bytes 6291456 | tf_op jit(solution)/shard_map/skc,sjc->kj/dot_general | solution.py:48
  289.7 3.9 copy.36
  293.7 7.9 %fusion.2 = bf16[1,1024,1024]{1,2,0:T(8,128)(2,1)} fusion(f32[1,1024,1024]{1,2,0:T(8,128)} %copy.29, bf16[1,1024,1024]{1,2,0:T(8,128)(2,1)} %copy.30, bf16[1024,1024]{1,0:T(8,128)(2,1)} %bitcast.29, bf16[1,1024,1024]{2,1,0:T(8,128)(2,1)} %param.6), kind=kOutput, calls=%fused_computation.5 | convolution fusion | flops 2151677952 | bytes 12582912 | tf_op jit(solution)/shard_map/kj,skc->sjc/dot_general | solution.py:57
  301.6 3.9 copy.37
  305.5 20.0 %reduce-scatter.5.cloned.1.call-done = bf16[128,1024]{1,0:T(8,128)(2,1)} async-done(((bf16[1024,1024]{1,0:T(8,128)(2,1)}), bf16[128,1024]{1,0:T(8,128)(2,1)}) %reduce-scatter.5.cloned.1.call-update) | async-done | bytes 262160 | tf_op jit(solution)/shard_map/reduce_scatter | solution.py:53
  327.3 93.9 %reduce-scatter.3.cloned.1.call-done = bf16[128,1024]{1,0:T(8,128)(2,1)} async-done(((bf16[1024,1024]{1,0:T(8,128)(2,1)}), bf16[128,1024]{1,0:T(8,128)(2,1)}) %reduce-scatter.3.cloned.1.call-update) | async-done | bytes 262160 | tf_op jit(solution)/shard_map/reduce_scatter | solution.py:50
  (14 shorter events, 6.2 us)
Async XLA Ops:
  7.2 62.6 %copy-start = (bf16[1,1024,1024]{2,1,0:T(8,128)(2,1)S(1)}, bf16[1,1024,1024]{2,1,0:T(8,128)(2,1)}, u32[]{:S(2)}) copy-start(bf16[1,1024,1024]{2,1,0:T(8,128)(2,1)} %param.7) | copy-start | bytes 6291460
  69.8 2.4 copy-start.1
  74.6 55.1 %all-to-all-start.1 = ((bf16[1,1,32,32,1024]{4,2,1,0,3:T(8,128)(2,1)}), bf16[1,1,32,32,1024]{4,2,1,0,3:T(8,128)(2,1)}, u32[]{:S(2)}, u32[]{:S(2)}) async-start(bf16[1,1,32,32,1024]{4,2,1,0,3:T(8,128)(2,1)} %copy.27), calls=%async_computation.1 | async-start | bytes 4194304 | tf_op jit(solution)/shard_map/all_to_all | solution.py:26
  205.4 2.5 copy-start.2
  210.3 73.4 %all-to-all-start.3 = ((bf16[1,1,32,32,1024]{4,2,1,0,3:T(8,128)(2,1)}), bf16[1,1,32,32,1024]{4,2,1,0,3:T(8,128)(2,1)}, u32[]{:S(2)}, u32[]{:S(2)}) async-start(bf16[1,1,32,32,1024]{4,2,1,0,3:T(8,128)(2,1)} %copy.35), calls=%async_computation.3 | async-start | bytes 4194304 | tf_op jit(solution)/shard_map/all_to_all | solution.py:37
  217.6 108.0 %reduce-scatter.5.cloned.1.call-start = ((), (), s32[]{:S(2)}) async-start(), calls=%async_computation.7 | async-start | bytes 2359296 | tf_op jit(solution)/shard_map/reduce_scatter | solution.py:53
  223.6 197.6 %reduce-scatter.3.cloned.1.call-start = ((), (), s32[]{:S(2)}) async-start(), calls=%async_computation.6 | async-start | bytes 2359296 | tf_op jit(solution)/shard_map/reduce_scatter | solution.py:50
Sparse Core Ops, SparseCore 0:
  223.7 101.8 reduce-scatter.4
  329.6 91.5 reduce-scatter.2
where the time goes:
time: 431 us; the launch traced here: 430 us
  waiting for transfers between devices  214 us (50%)
  blocking collectives  111 us (26%)
  local copies, waits for them, and re-layouts  32.3 us (7%)
  matrix products  29.2 us (7%)
  starting transfers between devices  14.7 us (3%)
  other arithmetic  14.5 us (3%)
  between operations  14.1 us (3%)
    reduce_scatter x1, waiting for transfers between devices, local(): lax.psum_scatter(part_one.astype(jnp.bfloat16), 'dp', scatter_dimension=0...  93.9 us
    all_to_all x1, waiting for transfers between devices, local(): lax.all_to_all(back_two.reshape(seqs, 1, rows, count, width), 'seq', spli...  59.9 us
    all_to_all x1, blocking collectives, local(): lax.all_to_all(first.reshape(seqs, count, rows, 1, width), 'seq', split_a...  56.7 us
    all_to_all x1, blocking collectives, local(): lax.all_to_all(gated.reshape(seqs, count, rows, 1, width), 'seq', split_a...  54.3 us
    all_to_all x1, waiting for transfers between devices, local(): lax.all_to_all(second.reshape(seqs, 1, rows, count, width), 'seq', split_...  40.1 us
    reduce_scatter x1, waiting for transfers between devices, local(): lax.psum_scatter(part_two.astype(jnp.bfloat16), 'dp', scatter_dimension=0...  20 us
    unnamed x10, local copies, waits for them, and re-layouts  15.8 us
  transfers between devices with their start and end apart: 4, of which 4 were waited for; matrix products, arithmetic and copies ran while one was open for 9% of the time, Pallas kernels for 0%

commit v1 on v0

--- a/solution.py
+++ b/solution.py
@@ -27,9 +27,16 @@
         second.reshape(seqs, 1, rows, count, width), "seq", split_axis=3, concat_axis=1, tiled=True
     )
     monarch = monarch.reshape(seqs, block, width)
-    gated_moved = lax.all_to_all(
-        gated.reshape(seqs, count, rows, 1, width), "seq", split_axis=1, concat_axis=3, tiled=True
-    )
+
+    def serve_the_limits(own_rows, link_axis):
+        return jnp.concatenate(
+            lax.all_to_all(
+                jnp.stack(jnp.split(own_rows, lax.axis_size(link_axis), 1)), link_axis, 0, 0
+            ),
+            axis=3,
+        )
+
+    gated_moved = serve_the_limits(gated.reshape(seqs, count, rows, 1, width), "seq")
     gated_moved = gated_moved.reshape(seqs, block, width)
     back_two = jnp.einsum(
         "pq,spc->sqc", ftwo, gated_moved, preferred_element_type=jnp.float32

time: 431 us -> 445 us (1.032)
  local copies, waits for them, and re-layouts: 32.3 us -> 46.1 us
    unnamed x10 -> x43, local copies, waits for them, and re-layouts: 15.8 us -> 29.5 us
  transfers between devices with their start and end apart: 4 -> 4, of which waited for: 4 -> 4; matrix products, arithmetic and copies ran while one was open for 9% -> 8% of each run, Pallas kernels for 0% -> 0%
where the time goes in v1:
time: 445 us; the launch traced here: 443 us
  waiting for transfers between devices  214 us (48%)
  blocking collectives  111 us (25%)
  local copies, waits for them, and re-layouts  46.1 us (10%)
  matrix products  29.3 us (7%)
  starting transfers between devices  14.6 us (3%)
  other arithmetic  14.5 us (3%)
  between operations  14.3 us (3%)
    reduce_scatter x1, waiting for transfers between devices, local(): lax.psum_scatter(part_one.astype(jnp.bfloat16), 'dp', scatter_dimension=0...  93.8 us
    all_to_all x1, waiting for transfers between devices, local(): lax.all_to_all(back_two.reshape(seqs, 1, rows, count, width), 'seq', spli...  59.9 us
    all_to_all x1, blocking collectives, local(): lax.all_to_all(first.reshape(seqs, count, rows, 1, width), 'seq', split_a...  56.7 us
    all_to_all x1, blocking collectives, serve_the_limits(): lax.all_to_all(jnp.stack(jnp.split(own_rows, lax.axis_size(link_axis), 1)...  54 us
    all_to_all x1, waiting for transfers between devices, local(): lax.all_to_all(second.reshape(seqs, 1, rows, count, width), 'seq', split_...  40.1 us
    unnamed x43, local copies, waits for them, and re-layouts  29.5 us
    reduce_scatter x1, waiting for transfers between devices, local(): lax.psum_scatter(part_two.astype(jnp.bfloat16), 'dp', scatter_dimension=0...  19.9 us
  transfers between devices with their start and end apart: 4, of which 4 were waited for; matrix products, arithmetic and copies ran while one was open for 8% of the time, Pallas kernels for 0%

profile of v1, /device:TPU:8, one launch (start us, length us, event | category | flops | bytes accessed | tf_op | source)
XLA Modules:
  0.0 443.2 jit_solution(1343551758639980163)
XLA Ops:
  7.2 4.7 %fusion.17 = bf16[1024,1024]{0,1:T(8,128)(2,1)S(1)} fusion(bf16[1,1024,1024]{2,1,0:T(8,128)(2,1)} %param.4, bf16[1,1024,1024]{2,1,0:T(8,128)(2,1)} %param.6), kind=kOutput, calls=%fused_computation.19 | convolution fusion | flops 2148532224 | bytes 6291456 | tf_op jit(solution)/shard_map/kj,sjc->skc/dot_general | solution.py:15
  11.9 56.7 %all_to_all.44 = bf16[1,32,32,1,1024]{4,2,3,0,1:T(8,128)(2,1)S(1)} all-to-all(bf16[1,32,32,1,1024]{4,2,3,0,1:T(8,128)(2,1)S(1)} %bitcast.276), channel_id=1, replica_groups=mesh['dp'=8,'seq'=32] {'seq'}, dimensions={1} | all-to-all | bytes 4194304 | tf_op jit(solution)/shard_map/all_to_all | solution.py:19
  69.8 2.4 fusion.22
  72.2 2.5 copy.88
  74.6 7.1 %all-to-all-start.1 = ((bf16[1,1,32,32,1024]{4,2,1,0,3:T(8,128)(2,1)}), bf16[1,1,32,32,1024]{4,2,1,0,3:T(8,128)(2,1)}, u32[]{:S(2)}, u32[]{:S(2)}) async-start(bf16[1,1,32,32,1024]{4,2,1,0,3:T(8,128)(2,1)} %copy.88), calls=%async_computation.1 | async-start | bytes 4194304 | tf_op jit(solution)/shard_map/all_to_all | solution.py:26
  81.8 3.9 copy.85
  85.7 3.9 copy.91
  89.6 40.1 %all-to-all-done.1 = bf16[1,1,32,32,1024]{4,2,1,0,3:T(8,128)(2,1)} async-done(((bf16[1,1,32,32,1024]{4,2,1,0,3:T(8,128)(2,1)}), bf16[1,1,32,32,1024]{4,2,1,0,3:T(8,128)(2,1)}, u32[]{:S(2)}, u32[]{:S(2)}) %all-to-all-start.1) | async-done | bytes 2097184 | tf_op jit(solution)/shard_map/all_to_all | solution.py:26
  129.7 4.1 bitcast_convert_fusion
  133.8 5.4 %copy.90 = f32[1,1024,1024]{1,2,0:T(8,128)} copy(f32[1,1024,1024]{2,1,0:T(8,128)} %bitcast.238) | data formatting | bytes 8388608 | tf_op jit(solution)/shard_map/convert_element_type | solution.py:52
  139.1 6.9 %fusion.3 = (bf16[1,1024,1024]{1,2,0:T(8,128)(2,1)}, bf16[1,1024,1024]{1,2,0:T(8,128)(2,1)}) fusion(bf16[1,1024,1024]{1,2,0:T(8,128)(2,1)} %copy.85, bf16[1,1024,1024]{1,2,0:T(8,128)(2,1)} %copy.91, f32[1,1024,1024]{1,2,0:T(8,128)} %copy.90), kind=kLoop, calls=%fused_computation.6 | loop fusion | flops 6291456 | bytes 12582912 | tf_op jit(solution)/shard_map/convert_element_type | solution.py:18
  146.0 3.9 copy.93
  163.8 54.0 %all_to_all.45 = bf16[32,1,1,32,1,1024]{5,3,4,2,1,0:T(8,128)(2,1)S(1)} all-to-all(bf16[32,1,1,32,1,1024]{5,3,4,2,1,0:T(8,128)(2,1)S(1)} %constant_dynamic-update-slice_fusion), channel_id=1, replica_groups=mesh['dp'=8,'seq'=32] {'seq'}, dimensions={0} | all-to-all | bytes 4194304 | tf_op jit(solution)/shard_map/all_to_all | solution.py:33
  219.0 2.4 fusion.25
  221.5 2.5 copy.125
  223.9 7.1 %all-to-all-start.3 = ((bf16[1,1,32,32,1024]{4,2,1,0,3:T(8,128)(2,1)}), bf16[1,1,32,32,1024]{4,2,1,0,3:T(8,128)(2,1)}, u32[]{:S(2)}, u32[]{:S(2)}) async-start(bf16[1,1,32,32,1024]{4,2,1,0,3:T(8,128)(2,1)} %copy.125), calls=%async_computation.3 | async-start | bytes 4194304 | tf_op jit(solution)/shard_map/all_to_all | solution.py:44
  231.2 5.9 %convolution_convert_fusion = bf16[1024,1024]{1,0:T(8,128)(2,1)} fusion(bf16[1024,1024]{1,0:T(8,128)(2,1)} %bitcast.275, bf16[1024,1024]{1,0:T(8,128)(2,1)} %bitcast.273), kind=kOutput, calls=%fused_computation.22 | convolution fusion | flops 2148532224 | bytes 6291456 | tf_op jit(solution)/shard_map/spc,sqc->pq/dot_general | solution.py:54
  237.4 59.9 %all-to-all-done.3 = bf16[1,1,32,32,1024]{4,2,1,0,3:T(8,128)(2,1)} async-done(((bf16[1,1,32,32,1024]{4,2,1,0,3:T(8,128)(2,1)}), bf16[1,1,32,32,1024]{4,2,1,0,3:T(8,128)(2,1)}, u32[]{:S(2)}, u32[]{:S(2)}) %all-to-all-start.3) | async-done | bytes 2097184 | tf_op jit(solution)/shard_map/all_to_all | solution.py:44
  297.3 6.0 %fusion.14 = bf16[1024,1024]{1,0:T(8,128)(2,1)} fusion(bf16[1024,1024]{1,0:T(8,128)(2,1)} %bitcast.89, bf16[1,1024,1024]{2,1,0:T(8,128)(2,1)} %param.4), kind=kOutput, calls=%fused_computation.18 | convolution fusion | flops 2148532224 | bytes 6291456 | tf_op jit(solution)/shard_map/skc,sjc->kj/dot_general | solution.py:55
  303.3 3.9 copy.126
  307.2 7.9 %fusion.2 = bf16[1,1024,1024]{1,2,0:T(8,128)(2,1)} fusion(f32[1,1024,1024]{1,2,0:T(8,128)} %copy.90, bf16[1,1024,1024]{1,2,0:T(8,128)(2,1)} %copy.91, bf16[1024,1024]{1,0:T(8,128)(2,1)} %bitcast.89, bf16[1,1024,1024]{2,1,0:T(8,128)(2,1)} %param.6), kind=kOutput, calls=%fused_computation.5 | convolution fusion | flops 2151677952 | bytes 12582912 | tf_op jit(solution)/shard_map/kj,skc->sjc/dot_general | solution.py:64
  315.1 3.9 copy.127
  319.1 19.9 %reduce-scatter.5.cloned.1.call-done = bf16[128,1024]{1,0:T(8,128)(2,1)} async-done(((bf16[1024,1024]{1,0:T(8,128)(2,1)}), bf16[128,1024]{1,0:T(8,128)(2,1)}) %reduce-scatter.5.cloned.1.call-update) | async-done | bytes 262160 | tf_op jit(solution)/shard_map/reduce_scatter | solution.py:60
  340.8 93.8 %reduce-scatter.3.cloned.1.call-done = bf16[128,1024]{1,0:T(8,128)(2,1)} async-done(((bf16[1024,1024]{1,0:T(8,128)(2,1)}), bf16[128,1024]{1,0:T(8,128)(2,1)}) %reduce-scatter.3.cloned.1.call-update) | async-done | bytes 262160 | tf_op jit(solution)/shard_map/reduce_scatter | solution.py:57
  (48 shorter events, 20.0 us)
Async XLA Ops:
  7.2 62.6 %copy-start = (bf16[1,1024,1024]{2,1,0:T(8,128)(2,1)S(1)}, bf16[1,1024,1024]{2,1,0:T(8,128)(2,1)}, u32[]{:S(2)}) copy-start(bf16[1,1024,1024]{2,1,0:T(8,128)(2,1)} %param.7) | copy-start | bytes 6291460
  69.8 2.4 copy-start.2
  74.6 55.1 %all-to-all-start.1 = ((bf16[1,1,32,32,1024]{4,2,1,0,3:T(8,128)(2,1)}), bf16[1,1,32,32,1024]{4,2,1,0,3:T(8,128)(2,1)}, u32[]{:S(2)}, u32[]{:S(2)}) async-start(bf16[1,1,32,32,1024]{4,2,1,0,3:T(8,128)(2,1)} %copy.88), calls=%async_computation.1 | async-start | bytes 4194304 | tf_op jit(solution)/shard_map/all_to_all | solution.py:26
  149.9 13.7 %copy-start.1 = (bf16[1,1024,1024]{2,1,0:T(8,128)(2,1)S(1)}, bf16[1,1024,1024]{2,1,0:T(8,128)(2,1)}, u32[]{:S(2)}) copy-start(bf16[1,1024,1024]{2,1,0:T(8,128)(2,1)} %copy.93) | copy-start | bytes 6291460
  219.0 2.5 copy-start.3
  223.9 73.3 %all-to-all-start.3 = ((bf16[1,1,32,32,1024]{4,2,1,0,3:T(8,128)(2,1)}), bf16[1,1,32,32,1024]{4,2,1,0,3:T(8,128)(2,1)}, u32[]{:S(2)}, u32[]{:S(2)}) async-start(bf16[1,1,32,32,1024]{4,2,1,0,3:T(8,128)(2,1)} %copy.125), calls=%async_computation.3 | async-start | bytes 4194304 | tf_op jit(solution)/shard_map/all_to_all | solution.py:44
  231.1 107.9 %reduce-scatter.5.cloned.1.call-start = ((), (), s32[]{:S(2)}) async-start(), calls=%async_computation.7 | async-start | bytes 2359296 | tf_op jit(solution)/shard_map/reduce_scatter | solution.py:60
  237.1 197.5 %reduce-scatter.3.cloned.1.call-start = ((), (), s32[]{:S(2)}) async-start(), calls=%async_computation.6 | async-start | bytes 2359296 | tf_op jit(solution)/shard_map/reduce_scatter | solution.py:57
Sparse Core Ops, SparseCore 0:
  237.2 101.7 reduce-scatter.4
  343.1 91.4 reduce-scatter.2
